TPU v7x, 32 devices: a whole 2x2x4 slice. The times are simulated.
32 devices in a mesh: shard: 8 (over z, x), tensor: 4 (over y, core).
Axes of the slice: x: 2, y: 2, z: 4, core: 2. Of those that a mesh axis runs over, the one named last changes fastest.
Arguments:
- wide_weight: bfloat16 [4, 4096, 4096], P(None, 'shard', 'tensor'), may hold values from -6 to 6
- wide_grad: bfloat16 [4, 4096, 4096], P(None, 'shard', 'tensor'), may hold values from -6 to 6
- wide_first: float32 [4, 4096, 256], P(None, ('shard', 'tensor')), may hold values from -4 to 4
- wide_second: float32 [4, 4096, 256], P(None, ('shard', 'tensor')), may hold values from 0.001 to 0.1
- wide_basis: bfloat16 [4, 4096, 256], P(None, 'tensor'), may hold values from -0.09375 to 0.09375
- narrow_weight: bfloat16 [4, 1024, 4096], P(None, 'shard', 'tensor'), may hold values from -6 to 6
- narrow_grad: bfloat16 [4, 1024, 4096], P(None, 'shard', 'tensor'), may hold values from -6 to 6
- narrow_first: float32 [4, 1024, 256], P(None, ('shard', 'tensor')), may hold values from -4 to 4
- narrow_second: float32 [4, 1024, 256], P(None, ('shard', 'tensor')), may hold values from 0.001 to 0.1
- narrow_basis: bfloat16 [4, 4096, 256], P(None, 'tensor'), may hold values from -0.09375 to 0.09375
- vocab_weight: bfloat16 [2, 32000, 4096], P(None, 'shard', 'tensor'), may hold values from -6 to 6
- vocab_grad: bfloat16 [2, 32000, 4096], P(None, 'shard', 'tensor'), may hold values from -6 to 6
- vocab_first: float32 [2, 32000, 256], P(None, ('shard', 'tensor')), may hold values from -4 to 4
- vocab_second: float32 [2, 32000, 256], P(None, ('shard', 'tensor')), may hold values from 0.001 to 0.1
- vocab_basis: bfloat16 [2, 4096, 256], P(None, 'tensor'), may hold values from -0.09375 to 0.09375
Outputs:
- wide_weight_new: bfloat16 [4, 4096, 4096], P(None, 'shard', 'tensor')
- wide_first_new: float32 [4, 4096, 256], P(None, ('shard', 'tensor'))
- wide_second_new: float32 [4, 4096, 256], P(None, ('shard', 'tensor'))
- narrow_weight_new: bfloat16 [4, 1024, 4096], P(None, 'shard', 'tensor')
- narrow_first_new: float32 [4, 1024, 256], P(None, ('shard', 'tensor'))
- narrow_second_new: float32 [4, 1024, 256], P(None, ('shard', 'tensor'))
- vocab_weight_new: bfloat16 [2, 32000, 4096], P(None, 'shard', 'tensor')
- vocab_first_new: float32 [2, 32000, 256], P(None, ('shard', 'tensor'))
- vocab_second_new: float32 [2, 32000, 256], P(None, ('shard', 'tensor'))
All inputs are finite; a program needn't handle non-finite values.
Results may differ from a plain program's by a relative error of at most 0.01.
Values may be sent and summed in bfloat16 or wider, within the bound.
No kernel may reach another device: no remote copies, remote signals or barrier semaphores. Data moves between devices by JAX's collectives and lax.ppermute only.
A program may use at most 192 MiB of HBM per device.

v0:
```python
import jax
import jax.numpy as jnp
from jax import lax
from jax.sharding import PartitionSpec as P

NS_ITERS = 3
HIGHEST = lax.Precision.HIGHEST


def local_gram(polish):
    return jnp.einsum("sdk,sdl->skl", polish, polish, precision=HIGHEST)


def polish_small(back, gram):
    trace = jnp.einsum("skk->s", gram)
    scale = 1.0 / jnp.sqrt(trace + 1e-06)
    small = gram * (scale * scale)[:, None, None]
    rank = gram.shape[1]
    eye = jnp.eye(rank, dtype=jnp.float32)[None, :, :]
    factor = jnp.broadcast_to(eye, gram.shape)
    for step in range(NS_ITERS):
        square = jnp.einsum("skl,slm->skm", small, small, precision=HIGHEST)
        turn = 3.4445 * eye - 4.775 * small + 2.0315 * square
        factor = jnp.einsum("skl,slm->skm", factor, turn, precision=HIGHEST)
        if step + 1 < NS_ITERS:
            small = jnp.einsum(
                "skl,slm->skm",
                turn,
                jnp.einsum("skl,slm->skm", small, turn, precision=HIGHEST),
                precision=HIGHEST,
            )
    return jnp.einsum("sdk,skl->sdl", back * scale[:, None, None], factor, precision=HIGHEST)


def adam_moments(first, second, projected):
    first_new = 0.9 * first + 0.1 * projected
    second_new = 0.999 * second + 0.001 * projected * projected
    direction = first_new / (1.0 - 0.9**10) / (jnp.sqrt(second_new / (1.0 - 0.999**10)) + 1e-08)
    return (first_new, second_new, direction.astype(jnp.bfloat16))


def per_device(
    wide_weight,
    wide_grad,
    wide_first,
    wide_second,
    wide_basis,
    narrow_weight,
    narrow_grad,
    narrow_first,
    narrow_second,
    narrow_basis,
    vocab_weight,
    vocab_grad,
    vocab_first,
    vocab_second,
    vocab_basis,
):
    weights = (wide_weight, narrow_weight, vocab_weight)
    grads = (wide_grad, narrow_grad, vocab_grad)
    firsts = (wide_first, narrow_first, vocab_first)
    seconds = (wide_second, narrow_second, vocab_second)
    olds = (wide_basis, narrow_basis, vocab_basis)
    sketch_terms = [
        jnp.einsum("smc,scr->smr", grad, old, preferred_element_type=jnp.float32)
        for grad, old in zip(grads, olds)
    ]
    sketch_sum = (
        lax.psum(sketch_terms[0].astype(jnp.bfloat16), "tensor").astype(jnp.float32),
        lax.psum(sketch_terms[1].astype(jnp.bfloat16), "tensor").astype(jnp.float32),
        lax.psum(sketch_terms[2].astype(jnp.bfloat16), "tensor").astype(jnp.float32),
    )
    sketches = [item.astype(jnp.bfloat16) for item in sketch_sum]
    back_terms = [
        jnp.einsum("smc,smr->scr", grad, sketch, preferred_element_type=jnp.float32)
        for grad, sketch in zip(grads, sketches)
    ]
    backs = (
        lax.psum_scatter(back_terms[0], "shard", scatter_dimension=1, tiled=True),
        lax.psum_scatter(back_terms[1], "shard", scatter_dimension=1, tiled=True),
        lax.psum_scatter(back_terms[2], "shard", scatter_dimension=1, tiled=True),
    )
    first_grams = lax.psum(tuple((local_gram(back) for back in backs)), ("shard", "tensor"))
    rounded = [
        polish_small(back, gram).astype(jnp.bfloat16) for back, gram in zip(backs, first_grams)
    ]
    bases = (
        lax.all_gather(rounded[0], "shard", axis=1, tiled=True),
        lax.all_gather(rounded[1], "shard", axis=1, tiled=True),
        lax.all_gather(rounded[2], "shard", axis=1, tiled=True),
    )
    proj_terms = [
        jnp.einsum("smc,scr->smr", grad, basis, preferred_element_type=jnp.float32)
        for grad, basis in zip(grads, bases)
    ]
    projected = (
        lax.psum_scatter(proj_terms[0], "tensor", scatter_dimension=1, tiled=True),
        lax.psum_scatter(proj_terms[1], "tensor", scatter_dimension=1, tiled=True),
        lax.psum_scatter(proj_terms[2], "tensor", scatter_dimension=1, tiled=True),
    )
    results = [
        adam_moments(first, second, proj) for first, second, proj in zip(firsts, seconds, projected)
    ]
    directions = (
        lax.all_gather(results[0][2], "tensor", axis=1, tiled=True),
        lax.all_gather(results[1][2], "tensor", axis=1, tiled=True),
        lax.all_gather(results[2][2], "tensor", axis=1, tiled=True),
    )
    outputs = []
    for weight, direction, basis, result in zip(weights, directions, bases, results):
        update = jnp.einsum("smr,scr->smc", direction, basis, preferred_element_type=jnp.float32)
        weight_new = (0.99 * weight.astype(jnp.float32) - 2.0 * update).astype(jnp.bfloat16)
        outputs.append((weight_new, result[0], result[1]))
    return (
        outputs[0][0],
        outputs[0][1],
        outputs[0][2],
        outputs[1][0],
        outputs[1][1],
        outputs[1][2],
        outputs[2][0],
        outputs[2][1],
        outputs[2][2],
    )


def solution(mesh):
    in_specs = (
        P(None, "shard", "tensor"),
        P(None, "shard", "tensor"),
        P(None, ("shard", "tensor"), None),
        P(None, ("shard", "tensor"), None),
        P(None, "tensor", None),
        P(None, "shard", "tensor"),
        P(None, "shard", "tensor"),
        P(None, ("shard", "tensor"), None),
        P(None, ("shard", "tensor"), None),
        P(None, "tensor", None),
        P(None, "shard", "tensor"),
        P(None, "shard", "tensor"),
        P(None, ("shard", "tensor"), None),
        P(None, ("shard", "tensor"), None),
        P(None, "tensor", None),
    )
    out_specs = (
        P(None, "shard", "tensor"),
        P(None, ("shard", "tensor"), None),
        P(None, ("shard", "tensor"), None),
        P(None, "shard", "tensor"),
        P(None, ("shard", "tensor"), None),
        P(None, ("shard", "tensor"), None),
        P(None, "shard", "tensor"),
        P(None, ("shard", "tensor"), None),
        P(None, ("shard", "tensor"), None),
    )
    return jax.shard_map(
        per_device, mesh=mesh, in_specs=in_specs, out_specs=out_specs, check_vma=False
    )
```

profile of v0, /device:TPU:0, one launch (start us, length us, event | category | flops | bytes accessed | tf_op | source)
XLA Modules:
  0.0 922.7 jit_solution(10910709305503595160)
XLA Ops:
  7.2 12.4 %convolution_convert_fusion = bf16[2,4000,256]{2,1,0:T(8,128)(2,1)} fusion(bf16[2,4000,1024]{2,1,0:T(8,128)(2,1)} %param.26, bf16[2,1024,256]{2,1,0:T(8,128)(2,1)} %param.29), kind=kOutput, calls=%fused_computation.3 | convolution fusion | flops 4196352000 | bytes 21528576 | tf_op jit(solution)/shard_map/smc,scr->smr/dot_general | solution.py:65
  19.7 4.6 convolution_convert_fusion.1
  24.3 1.6 convolution_convert_fusion.3
  26.0 108.4 %all-reduce.11.cloned.1.call-done = (bf16[4,512,256]{1,2,0:T(8,128)(2,1)}, bf16[4,128,256]{1,2,0:T(8,128)(2,1)}, bf16[2,4000,256]{2,1,0:T(8,128)(2,1)}) async-done(((bf16[4,512,256]{1,2,0:T(8,128)(2,1)}, bf16[4,128,256]{1,2,0:T(8,128)(2,1)}, bf16[2,4000,256]{2,1,0:T(8,128)(2,1)}), (bf16[4,512,256]{1,2,0:T(8,128)(2,1)}, bf16[4,128,256]{1,2,0:T(8,128)(2,1)}, ...) | async-done | bytes 5406736 | tf_op jit(solution)/shard_map/psum | solution.py:69
  134.3 12.8 %convolution_bitcast_fusion.3 = f32[2,1024,256]{1,2,0:T(8,128)} fusion(bf16[2,4000,256]{2,1,0:T(8,128)(2,1)} %get-tuple-element.34, bf16[2,4000,1024]{2,1,0:T(8,128)(2,1)} %param.26), kind=kOutput, calls=%fused_computation.11 | convolution fusion | flops 4194304000 | bytes 22577152 | tf_op jit(solution)/shard_map/smc,smr->scr/dot_general | solution.py:75
  148.4 5.5 convolution_bitcast_fusion.2
  154.8 2.7 convolution_bitcast_fusion.1
  157.6 58.0 %reduce-scatter.12.cloned.1.call-done = f32[2,128,256]{1,2,0:T(8,128)} async-done(((f32[2,1024,256]{1,2,0:T(8,128)}), f32[2,128,256]{1,2,0:T(8,128)}) %reduce-scatter.12.cloned.1.call-update) | async-done | bytes 262160 | tf_op jit(solution)/shard_map/reduce_scatter | solution.py:81
  215.6 2.4 fusion.63
  218.0 89.7 %reduce-scatter.6.cloned.1.call-done = f32[4,128,256]{1,2,0:T(8,128)} async-done(((f32[4,1024,256]{1,2,0:T(8,128)}), f32[4,128,256]{1,2,0:T(8,128)}) %reduce-scatter.6.cloned.1.call-update) | async-done | bytes 524304 | tf_op jit(solution)/shard_map/reduce_scatter | solution.py:79
  307.7 3.2 fusion.51
  310.8 89.0 %reduce-scatter.10.cloned.1.call-done = f32[4,128,256]{1,2,0:T(8,128)} async-done(((f32[4,1024,256]{1,2,0:T(8,128)}), f32[4,128,256]{1,2,0:T(8,128)}) %reduce-scatter.10.cloned.1.call-update) | async-done | bytes 524304 | tf_op jit(solution)/shard_map/reduce_scatter | solution.py:80
  399.8 3.2 fusion.57
  403.2 141.4 %all-reduce.9.cloned.1.call-done = (f32[4,256,256]{2,1,0:T(8,128)}, f32[4,256,256]{2,1,0:T(8,128)}, f32[2,256,256]{2,1,0:T(8,128)}) async-done(((f32[4,256,256]{2,1,0:T(8,128)}, f32[4,256,256]{2,1,0:T(8,128)}, f32[2,256,256]{2,1,0:T(8,128)}), (f32[4,256,256]{2,1,0:T(8,128)}, f32[4,256,256]{2,1,0:T(8,128)}, f32[2,256,256]{2,1,0:T(8,128)})) %all-reduce.9.cloned.1.call-update) | async-done | bytes 2621456 | tf_op jit(solution)/shard_map/psum | solution.py:83
  544.5 1.4 select_reduce_fusion.2
  545.9 2.2 fusion.9
  548.1 1.6 select_reduce_fusion
  549.7 1.4 fusion.6
  551.2 1.2 fusion.14
  553.5 1.3 fusion.5
  557.1 1.3 fusion.4
  559.5 1.3 fusion.53
  562.0 1.8 convolution_convert_fusion.4
  569.9 1.4 convolution_convert_fusion.5
  571.3 1.4 fusion.3
  572.7 1.2 fusion.11
  575.0 1.2 fusion.2
  576.6 2.0 fusion.22
  582.0 1.3 fusion.1
  584.5 1.8 convolution_convert_fusion.2
  586.4 25.7 %all-gather.6.cloned.1.call-done = bf16[4,1024,256]{2,1,0:T(8,128)(2,1)} async-done(((bf16[4,128,256]{2,1,0:T(8,128)(2,1)}), bf16[4,1024,256]{2,1,0:T(8,128)(2,1)}) %all-gather.6.cloned.1.call-update) | async-done | bytes 2097168 | tf_op jit(solution)/shard_map/all_gather | solution.py:88
  612.2 5.5 convolution_bitcast_fusion.4
  618.2 35.5 %all-gather.12.cloned.1.call-done = bf16[2,1024,256]{2,1,0:T(8,128)(2,1)} async-done(((bf16[2,128,256]{2,1,0:T(8,128)(2,1)}), bf16[2,1024,256]{2,1,0:T(8,128)(2,1)}) %all-gather.12.cloned.1.call-update) | async-done | bytes 1048592 | tf_op jit(solution)/shard_map/all_gather | solution.py:90
  653.6 13.6 %convolution_bitcast_fusion = f32[2,4000,256]{2,1,0:T(8,128)} fusion(bf16[2,4000,1024]{2,1,0:T(8,128)(2,1)} %param.26, bf16[2,1024,256]{2,1,0:T(8,128)(2,1)} %all-gather.12.cloned.1.call-done), kind=kOutput, calls=%fused_computation.2 | convolution fusion | flops 4194304000 | bytes 25624576 | tf_op jit(solution)/shard_map/smc,scr->smr/dot_general | solution.py:93
  669.5 34.9 %all-gather.10.cloned.1.call-done = bf16[4,1024,256]{2,1,0:T(8,128)(2,1)} async-done(((bf16[4,128,256]{2,1,0:T(8,128)(2,1)}), bf16[4,1024,256]{2,1,0:T(8,128)(2,1)}) %all-gather.10.cloned.1.call-update) | async-done | bytes 2097168 | tf_op jit(solution)/shard_map/all_gather | solution.py:89
  704.4 2.4 convolution_bitcast_fusion.5
  708.0 29.6 %reduce-scatter.8.cloned.1.call-done = f32[4,128,256]{1,2,0:T(8,128)} async-done(((f32[4,512,256]{1,2,0:T(8,128)}), f32[4,128,256]{1,2,0:T(8,128)}) %reduce-scatter.8.cloned.1.call-update) | async-done | bytes 524304 | tf_op jit(solution)/shard_map/reduce_scatter | solution.py:97
  737.5 2.3 divide_convert_fusion.1
  739.9 71.4 %reduce-scatter.14.cloned.1.call-done = f32[2,1000,256]{2,1,0:T(8,128)} async-done(((f32[2,4000,256]{2,1,0:T(8,128)}), f32[2,1000,256]{2,1,0:T(8,128)}) %reduce-scatter.14.cloned.1.call-update) | async-done | bytes 2048016 | tf_op jit(solution)/shard_map/reduce_scatter | solution.py:99
  811.3 6.0 divide_convert_fusion
  818.6 29.0 %all-reduce.7.cloned.1.call-done = f32[4,128,256]{2,0,1:T(4,128)} async-done(((f32[4,128,256]{2,0,1:T(4,128)}), f32[4,128,256]{2,0,1:T(4,128)}) %all-reduce.7.cloned.1.call-update) | async-done | bytes 524304
  847.5 1.2 fusion.43
  850.1 5.9 all_gather.21
  856.1 3.0 subtract_convert_fusion.2
  861.1 5.4 all-gather.8.cloned.1.call-done
  866.5 6.4 subtract_convert_fusion.1
  872.9 29.8 %all-gather.14.cloned.1.call-done = bf16[2,4000,256]{2,1,0:T(8,128)(2,1)} async-done(((bf16[2,1000,256]{2,1,0:T(8,128)(2,1)}), bf16[2,4000,256]{2,1,0:T(8,128)(2,1)}) %all-gather.14.cloned.1.call-update) | async-done | bytes 4096016 | tf_op jit(solution)/shard_map/all_gather | solution.py:107
  902.7 13.3 %subtract_convert_fusion = bf16[2,4000,1024]{2,1,0:T(8,128)(2,1)} fusion(bf16[2,4000,1024]{2,1,0:T(8,128)(2,1)} %param.25, bf16[2,4000,256]{2,1,0:T(8,128)(2,1)} %all-gather.14.cloned.1.call-done, bf16[2,1024,256]{2,1,0:T(8,128)(2,1)S(1)} %copy-done.20), kind=kOutput, calls=%fused_computation | convolution fusion | flops 4235264000 | bytes 37912576 | tf_op jit(solution)/shard_map/smr,scr->smc/dot_general | solution.py:111
  (102 shorter events, 28.0 us)
Async XLA Ops:
  7.2 12.5 %copy-start = (bf16[4,1024,256]{2,1,0:T(8,128)(2,1)S(1)}, bf16[4,1024,256]{2,1,0:T(8,128)(2,1)}, u32[]{:S(2)}) copy-start(bf16[4,1024,256]{2,1,0:T(8,128)(2,1)} %param.19) | copy-start | bytes 6291460
  7.2 127.1 %all-reduce.11.cloned.1.call-start = ((), (), s32[]{:S(2)}) async-start(), calls=%async_computation.17 | async-start | bytes 10813440 | tf_op jit(solution)/shard_map/psum | solution.py:69
  19.7 4.6 copy-start.2
  19.7 4.6 copy-start.12
  25.9 189.7 %reduce-scatter.12.cloned.1.call-start = ((), (), s32[]{:S(2)}) async-start(), calls=%async_computation.11 | async-start | bytes 2359296 | tf_op jit(solution)/shard_map/reduce_scatter | solution.py:81
  147.1 1.2 copy-start.14
  147.2 160.5 %reduce-scatter.6.cloned.1.call-start = ((), (), s32[]{:S(2)}) async-start(), calls=%async_computation.5 | async-start | bytes 4718592 | tf_op jit(solution)/shard_map/reduce_scatter | solution.py:79
  153.8 1.0 copy-start.17
  153.9 246.0 %reduce-scatter.10.cloned.1.call-start = ((), (), s32[]{:S(2)}) async-start(), calls=%async_computation.9 | async-start | bytes 4718592 | tf_op jit(solution)/shard_map/reduce_scatter | solution.py:80
  157.6 387.0 %all-reduce.9.cloned.1.call-start = ((), (), s32[]{:S(2)}) async-start(), calls=%async_computation.16 | async-start | bytes 5242880 | tf_op jit(solution)/shard_map/psum | solution.py:83
  403.0 209.1 %all-gather.6.cloned.1.call-start = ((), (), s32[]{:S(2)}) async-start(), calls=%async_computation.6 | async-start | bytes 2359296 | tf_op jit(solution)/shard_map/all_gather | solution.py:88
  403.1 160.8 %copy-start.10 = (f32[256,256]{1,0:T(8,128)}, f32[256,256]{1,0:T(8,128)S(1)}, u32[]{:S(2)}) copy-start(f32[256,256]{1,0:T(8,128)S(1)} %fusion.38) | copy-start | bytes 786436
  544.5 3.6 copy-start.4
  544.5 5.2 copy-start.5
  560.8 1.2 copy-start.9
  562.0 2.6 copy-start.7
  563.9 89.8 %all-gather.12.cloned.1.call-start = ((), (), s32[]{:S(2)}) async-start(), calls=%async_computation.12 | async-start | bytes 1179648 | tf_op jit(solution)/shard_map/all_gather | solution.py:90
  568.6 1.4 copy-start.11
  576.3 128.1 %all-gather.10.cloned.1.call-start = ((), (), s32[]{:S(2)}) async-start(), calls=%async_computation.10 | async-start | bytes 2359296 | tf_op jit(solution)/shard_map/all_gather | solution.py:89
  583.3 1.2 copy-start.8
  586.4 151.1 %reduce-scatter.8.cloned.1.call-start = ((), (), s32[]{:S(2)}) async-start(), calls=%async_computation.7 | async-start | bytes 2621440 | tf_op jit(solution)/shard_map/reduce_scatter | solution.py:97
  617.7 193.5 %reduce-scatter.14.cloned.1.call-start = ((), (), s32[]{:S(2)}) async-start(), calls=%async_computation.13 | async-start | bytes 10240000 | tf_op jit(solution)/shard_map/reduce_scatter | solution.py:99
  667.3 1.0 copy-start.15
  667.3 1.2 copy-start.16
  667.3 37.1 %copy-start.3 = (bf16[4,128,1024]{2,1,0:T(8,128)(2,1)S(1)}, bf16[4,128,1024]{2,1,0:T(8,128)(2,1)}, u32[]{:S(2)}) copy-start(bf16[4,128,1024]{2,1,0:T(8,128)(2,1)} %param.21) | copy-start | bytes 3145732
  667.3 180.2 %all-reduce.7.cloned.1.call-start = ((), (), s32[]{:S(2)}) async-start(), calls=%async_computation.15 | async-start | bytes 1048576
  707.9 158.6 %all-gather.8.cloned.1.call-start = ((), (), s32[]{:S(2)}) async-start(), calls=%async_computation.8 | async-start | bytes 1310720 | tf_op jit(solution)/shard_map/all_gather | solution.py:105
  739.8 77.5 %copy-start.21 = (u32[32]{0:T(128)S(1)}, u32[32]{0:T(128)}, u32[]{:S(2)}) copy-start(u32[32]{0:T(128)} %constant.11) | copy-start | bytes 388
  739.8 107.7 %copy-start.18 = (f32[4,32,256]{2,1,0:T(8,128)S(1)}, f32[4,32,256]{2,1,0:T(8,128)}, u32[]{:S(2)}) copy-start(f32[4,32,256]{2,1,0:T(8,128)} %param.22) | copy-start | bytes 393220
  739.8 107.7 %copy-start.19 = (f32[4,32,256]{2,1,0:T(8,128)S(1)}, f32[4,32,256]{2,1,0:T(8,128)}, u32[]{:S(2)}) copy-start(f32[4,32,256]{2,1,0:T(8,128)} %param.23) | copy-start | bytes 393220
  739.8 162.8 %all-gather.14.cloned.1.call-start = ((), (), s32[]{:S(2)}) async-start(), calls=%async_computation.14 | async-start | bytes 5120000 | tf_op jit(solution)/shard_map/all_gather | solution.py:107
  817.3 38.8 %copy-start.6 = (bf16[4,1024,256]{2,1,0:T(8,128)(2,1)S(1)}, bf16[4,1024,256]{2,1,0:T(8,128)(2,1)}, u32[]{:S(2)}) copy-start(bf16[4,1024,256]{2,1,0:T(8,128)(2,1)} %all-gather.10.cloned.1.call-done) | copy-start | bytes 6291460
  859.1 7.4 copy-start.13
  861.1 41.6 %copy-start.20 = (bf16[2,1024,256]{2,1,0:T(8,128)(2,1)S(1)}, bf16[2,1024,256]{2,1,0:T(8,128)(2,1)}, u32[]{:S(2)}) copy-start(bf16[2,1024,256]{2,1,0:T(8,128)(2,1)} %all-gather.12.cloned.1.call-done) | copy-start | bytes 3145732
  902.6 13.3 %copy-start.1 = (bf16[4,1024,256]{2,1,0:T(8,128)(2,1)S(1)}, bf16[4,1024,256]{2,1,0:T(8,128)(2,1)}, u32[]{:S(2)}) copy-start(bf16[4,1024,256]{2,1,0:T(8,128)(2,1)} %param.19) | copy-start | bytes 6291460
Sparse Core Ops, SparseCore 0:
  26.0 108.2 all-reduce.10
  147.3 68.2 reduce-scatter.11
  220.2 87.4 reduce-scatter.5
  311.7 88.0 reduce-scatter.9
  407.6 136.8 all-reduce.8
  564.0 48.1 all-gather.5
  614.9 38.6 all-gather.11
  656.4 48.0 all-gather.9
  707.5 29.9 reduce-scatter.7
  740.8 70.4 reduce-scatter.13
  814.3 33.1 all-reduce.6
  849.6 16.8 all-gather.7
  868.7 33.9 all-gather.13
where the time goes:
time: 931 us; the launch traced here: 923 us
  waiting for transfers between devices  748 us (80%)
  matrix products  131 us (14%)
  between operations  15.2 us (2%)
  other arithmetic  12.5 us (1%)
    psum x1, waiting for transfers between devices, per_device(): lax.psum(tuple((local_gram(back) for back in backs)), ('shard', 'tensor'))  141 us
    psum x1, waiting for transfers between devices, per_device(): lax.psum(sketch_terms[0].astype(jnp.bfloat16), 'tensor').astype(jnp.float32)  108 us
    reduce_scatter x1, waiting for transfers between devices, per_device(): lax.psum_scatter(back_terms[0], 'shard', scatter_dimension=1, tiled=True)  89.7 us
    reduce_scatter x1, waiting for transfers between devices, per_device(): lax.psum_scatter(back_terms[1], 'shard', scatter_dimension=1, tiled=True)  89 us
    reduce_scatter x1, waiting for transfers between devices, per_device(): lax.psum_scatter(proj_terms[2], 'tensor', scatter_dimension=1, tiled=True)  71.4 us
    reduce_scatter x1, waiting for transfers between devices, per_device(): lax.psum_scatter(back_terms[2], 'shard', scatter_dimension=1, tiled=True)  58 us
    all_gather x1, waiting for transfers between devices, per_device(): lax.all_gather(rounded[2], 'shard', axis=1, tiled=True)  35.5 us
    all_gather x1, waiting for transfers between devices, per_device(): lax.all_gather(rounded[1], 'shard', axis=1, tiled=True)  34.9 us
  transfers between devices with their start and end apart: 13, of which 13 were waited for; matrix products, arithmetic and copies ran while one was open for 9% of the time, Pallas kernels for 0%

commit v1 on v0

--- a/solution.py
+++ b/solution.py
@@ -80,7 +80,7 @@
         lax.psum_scatter(back_terms[1], "shard", scatter_dimension=1, tiled=True),
         lax.psum_scatter(back_terms[2], "shard", scatter_dimension=1, tiled=True),
     )
-    first_grams = lax.psum(tuple((local_gram(back) for back in backs)), ("shard", "tensor"))
+    first_grams = lax.psum(lax.psum(tuple((local_gram(back) for back in backs)), "tensor"), "shard")
     rounded = [
         polish_small(back, gram).astype(jnp.bfloat16) for back, gram in zip(backs, first_grams)
     ]

time: 931 us -> 972 us (1.044)
  waiting for transfers between devices: 748 us -> 788 us
    psum x1 -> x2, waiting for transfers between devices: 141 us -> 181 us  [the longest x1 121 us: per_device(): lax.psum(lax.psum(tuple((local_gram(back) for back in backs)), 'tensor'),...]
    unnamed x14 -> x15, waiting for transfers between devices: 29.2 us -> 29 us
  transfers between devices with their start and end apart: 13 -> 14, of which waited for: 13 -> 14; matrix products, arithmetic and copies ran while one was open for 9% -> 9% of each run, Pallas kernels for 0% -> 0%
where the time goes in v1:
time: 972 us; the launch traced here: 963 us
  waiting for transfers between devices  788 us (81%)
  matrix products  131 us (13%)
  between operations  15.2 us (2%)
  other arithmetic  12.5 us (1%)
    psum x1, waiting for transfers between devices, per_device(): lax.psum(lax.psum(tuple((local_gram(back) for back in backs)), 'tensor'),...  121 us
    psum x1, waiting for transfers between devices, per_device(): lax.psum(sketch_terms[0].astype(jnp.bfloat16), 'tensor').astype(jnp.float32)  108 us
    reduce_scatter x1, waiting for transfers between devices, per_device(): lax.psum_scatter(back_terms[0], 'shard', scatter_dimension=1, tiled=True)  89.7 us
    reduce_scatter x1, waiting for transfers between devices, per_device(): lax.psum_scatter(back_terms[1], 'shard', scatter_dimension=1, tiled=True)  89 us
    reduce_scatter x1, waiting for transfers between devices, per_device(): lax.psum_scatter(proj_terms[2], 'tensor', scatter_dimension=1, tiled=True)  71.4 us
    psum x1, waiting for transfers between devices, per_device(): lax.psum(tuple((local_gram(back) for back in backs)), 'tensor')  60.5 us
    reduce_scatter x1, waiting for transfers between devices, per_device(): lax.psum_scatter(back_terms[2], 'shard', scatter_dimension=1, tiled=True)  58 us
    all_gather x1, waiting for transfers between devices, per_device(): lax.all_gather(rounded[2], 'shard', axis=1, tiled=True)  35.7 us
  transfers between devices with their start and end apart: 14, of which 14 were waited for; matrix products, arithmetic and copies ran while one was open for 9% of the time, Pallas kernels for 0%

profile of v1, /device:TPU:0, one launch (start us, length us, event | category | flops | bytes accessed | tf_op | source)
XLA Modules:
  0.0 963.1 jit_solution(6798096311011465155)
XLA Ops:
  7.2 12.4 %convolution_convert_fusion = bf16[2,4000,256]{2,1,0:T(8,128)(2,1)} fusion(bf16[2,4000,1024]{2,1,0:T(8,128)(2,1)} %param.26, bf16[2,1024,256]{2,1,0:T(8,128)(2,1)} %param.29), kind=kOutput, calls=%fused_computation.3 | convolution fusion | flops 4196352000 | bytes 21528576 | tf_op jit(solution)/shard_map/smc,scr->smr/dot_general | solution.py:65
  19.7 4.6 convolution_convert_fusion.1
  24.3 1.6 convolution_convert_fusion.3
  26.0 108.4 %all-reduce.15.cloned.1.call-done = (bf16[4,512,256]{1,2,0:T(8,128)(2,1)}, bf16[4,128,256]{1,2,0:T(8,128)(2,1)}, bf16[2,4000,256]{2,1,0:T(8,128)(2,1)}) async-done(((bf16[4,512,256]{1,2,0:T(8,128)(2,1)}, bf16[4,128,256]{1,2,0:T(8,128)(2,1)}, bf16[2,4000,256]{2,1,0:T(8,128)(2,1)}), (bf16[4,512,256]{1,2,0:T(8,128)(2,1)}, bf16[4,128,256]{1,2,0:T(8,128)(2,1)}, ...) | async-done | bytes 5406736 | tf_op jit(solution)/shard_map/psum | solution.py:69
  134.3 12.8 %convolution_bitcast_fusion.3 = f32[2,1024,256]{1,2,0:T(8,128)} fusion(bf16[2,4000,256]{2,1,0:T(8,128)(2,1)} %get-tuple-element.37, bf16[2,4000,1024]{2,1,0:T(8,128)(2,1)} %param.26), kind=kOutput, calls=%fused_computation.11 | convolution fusion | flops 4194304000 | bytes 22577152 | tf_op jit(solution)/shard_map/smc,smr->scr/dot_general | solution.py:75
  148.4 5.5 convolution_bitcast_fusion.2
  154.8 2.7 convolution_bitcast_fusion.1
  157.6 58.0 %reduce-scatter.12.cloned.1.call-done = f32[2,128,256]{1,2,0:T(8,128)} async-done(((f32[2,1024,256]{1,2,0:T(8,128)}), f32[2,128,256]{1,2,0:T(8,128)}) %reduce-scatter.12.cloned.1.call-update) | async-done | bytes 262160 | tf_op jit(solution)/shard_map/reduce_scatter | solution.py:81
  215.6 2.4 fusion.63
  218.0 89.7 %reduce-scatter.6.cloned.1.call-done = f32[4,128,256]{1,2,0:T(8,128)} async-done(((f32[4,1024,256]{1,2,0:T(8,128)}), f32[4,128,256]{1,2,0:T(8,128)}) %reduce-scatter.6.cloned.1.call-update) | async-done | bytes 524304 | tf_op jit(solution)/shard_map/reduce_scatter | solution.py:79
  307.7 3.2 fusion.51
  310.9 89.0 %reduce-scatter.10.cloned.1.call-done = f32[4,128,256]{1,2,0:T(8,128)} async-done(((f32[4,1024,256]{1,2,0:T(8,128)}), f32[4,128,256]{1,2,0:T(8,128)}) %reduce-scatter.10.cloned.1.call-update) | async-done | bytes 524304 | tf_op jit(solution)/shard_map/reduce_scatter | solution.py:80
  399.8 3.2 fusion.57
  403.1 60.5 %all-reduce.13.cloned.1.call-done = (f32[4,256,256]{2,1,0:T(8,128)}, f32[4,256,256]{2,1,0:T(8,128)}, f32[2,256,256]{2,1,0:T(8,128)}) async-done(((f32[4,256,256]{2,1,0:T(8,128)}, f32[4,256,256]{2,1,0:T(8,128)}, f32[2,256,256]{2,1,0:T(8,128)}), (f32[4,256,256]{2,1,0:T(8,128)}, f32[4,256,256]{2,1,0:T(8,128)}, f32[2,256,256]{2,1,0:T(8,128)})) %all-reduce.13.cloned.1.call-update) | async-done | bytes 2621456 | tf_op jit(solution)/shard_map/psum | solution.py:83
  463.8 120.8 %all-reduce.11.cloned.1.call-done = (f32[4,256,256]{2,1,0:T(8,128)}, f32[4,256,256]{2,1,0:T(8,128)}, f32[2,256,256]{2,1,0:T(8,128)}) async-done(((f32[4,256,256]{2,1,0:T(8,128)}, f32[4,256,256]{2,1,0:T(8,128)}, f32[2,256,256]{2,1,0:T(8,128)}), (f32[4,256,256]{2,1,0:T(8,128)}, f32[4,256,256]{2,1,0:T(8,128)}, f32[2,256,256]{2,1,0:T(8,128)})) %all-reduce.11.cloned.1.call-update) | async-done | bytes 2621456 | tf_op jit(solution)/shard_map/psum | solution.py:83
  584.6 1.4 select_reduce_fusion.2
  586.0 2.2 fusion.9
  588.2 1.6 select_reduce_fusion
  589.8 1.4 fusion.6
  591.2 1.2 fusion.14
  593.6 1.3 fusion.5
  597.2 1.3 fusion.4
  599.6 1.3 fusion.53
  602.1 1.8 convolution_convert_fusion.4
  610.0 1.4 convolution_convert_fusion.5
  611.4 1.4 fusion.3
  615.1 1.2 fusion.2
  616.7 2.0 fusion.22
  622.1 1.3 fusion.1
  624.6 1.8 convolution_convert_fusion.2
  626.5 26.0 %all-gather.6.cloned.1.call-done = bf16[4,1024,256]{2,1,0:T(8,128)(2,1)} async-done(((bf16[4,128,256]{2,1,0:T(8,128)(2,1)}), bf16[4,1024,256]{2,1,0:T(8,128)(2,1)}) %all-gather.6.cloned.1.call-update) | async-done | bytes 2097168 | tf_op jit(solution)/shard_map/all_gather | solution.py:88
  652.5 5.5 convolution_bitcast_fusion.4
  658.6 35.7 %all-gather.12.cloned.1.call-done = bf16[2,1024,256]{2,1,0:T(8,128)(2,1)} async-done(((bf16[2,128,256]{2,1,0:T(8,128)(2,1)}), bf16[2,1024,256]{2,1,0:T(8,128)(2,1)}) %all-gather.12.cloned.1.call-update) | async-done | bytes 1048592 | tf_op jit(solution)/shard_map/all_gather | solution.py:90
  694.2 13.6 %convolution_bitcast_fusion = f32[2,4000,256]{2,1,0:T(8,128)} fusion(bf16[2,4000,1024]{2,1,0:T(8,128)(2,1)} %param.26, bf16[2,1024,256]{2,1,0:T(8,128)(2,1)} %all-gather.12.cloned.1.call-done), kind=kOutput, calls=%fused_computation.2 | convolution fusion | flops 4194304000 | bytes 25624576 | tf_op jit(solution)/shard_map/smc,scr->smr/dot_general | solution.py:93
  710.1 35.2 %all-gather.10.cloned.1.call-done = bf16[4,1024,256]{2,1,0:T(8,128)(2,1)} async-done(((bf16[4,128,256]{2,1,0:T(8,128)(2,1)}), bf16[4,1024,256]{2,1,0:T(8,128)(2,1)}) %all-gather.10.cloned.1.call-update) | async-done | bytes 2097168 | tf_op jit(solution)/shard_map/all_gather | solution.py:89
  745.3 2.4 convolution_bitcast_fusion.5
  748.8 29.5 %reduce-scatter.8.cloned.1.call-done = f32[4,128,256]{1,2,0:T(8,128)} async-done(((f32[4,512,256]{1,2,0:T(8,128)}), f32[4,128,256]{1,2,0:T(8,128)}) %reduce-scatter.8.cloned.1.call-update) | async-done | bytes 524304 | tf_op jit(solution)/shard_map/reduce_scatter | solution.py:97
  778.4 2.3 divide_convert_fusion.1
  780.7 71.4 %reduce-scatter.14.cloned.1.call-done = f32[2,1000,256]{2,1,0:T(8,128)} async-done(((f32[2,4000,256]{2,1,0:T(8,128)}), f32[2,1000,256]{2,1,0:T(8,128)}) %reduce-scatter.14.cloned.1.call-update) | async-done | bytes 2048016 | tf_op jit(solution)/shard_map/reduce_scatter | solution.py:99
  852.1 6.0 divide_convert_fusion
  859.4 28.7 %all-reduce.9.cloned.1.call-done = f32[4,128,256]{2,0,1:T(4,128)} async-done(((f32[4,128,256]{2,0,1:T(4,128)}), f32[4,128,256]{2,0,1:T(4,128)}) %all-reduce.9.cloned.1.call-update) | async-done | bytes 524304
  888.2 1.2 fusion.43
  890.7 5.9 all_gather.21
  896.7 3.0 subtract_convert_fusion.2
  901.7 5.4 all-gather.8.cloned.1.call-done
  907.2 6.4 subtract_convert_fusion.1
  913.6 29.5 %all-gather.14.cloned.1.call-done = bf16[2,4000,256]{2,1,0:T(8,128)(2,1)} async-done(((bf16[2,1000,256]{2,1,0:T(8,128)(2,1)}), bf16[2,4000,256]{2,1,0:T(8,128)(2,1)}) %all-gather.14.cloned.1.call-update) | async-done | bytes 4096016 | tf_op jit(solution)/shard_map/all_gather | solution.py:107
  943.1 13.3 %subtract_convert_fusion = bf16[2,4000,1024]{2,1,0:T(8,128)(2,1)} fusion(bf16[2,4000,1024]{2,1,0:T(8,128)(2,1)} %param.25, bf16[2,4000,256]{2,1,0:T(8,128)(2,1)} %all-gather.14.cloned.1.call-done, bf16[2,1024,256]{2,1,0:T(8,128)(2,1)S(1)} %copy-done.20), kind=kOutput, calls=%fused_computation | convolution fusion | flops 4235264000 | bytes 37912576 | tf_op jit(solution)/shard_map/smr,scr->smc/dot_general | solution.py:111
  (105 shorter events, 29.2 us)
Async XLA Ops:
  7.2 12.5 %copy-start = (bf16[4,1024,256]{2,1,0:T(8,128)(2,1)S(1)}, bf16[4,1024,256]{2,1,0:T(8,128)(2,1)}, u32[]{:S(2)}) copy-start(bf16[4,1024,256]{2,1,0:T(8,128)(2,1)} %param.19) | copy-start | bytes 6291460
  7.2 127.1 %all-reduce.15.cloned.1.call-start = ((), (), s32[]{:S(2)}) async-start(), calls=%async_computation.18 | async-start | bytes 10813440 | tf_op jit(solution)/shard_map/psum | solution.py:69
  19.7 4.6 copy-start.2
  19.7 4.6 copy-start.12
  25.9 189.7 %reduce-scatter.12.cloned.1.call-start = ((), (), s32[]{:S(2)}) async-start(), calls=%async_computation.11 | async-start | bytes 2359296 | tf_op jit(solution)/shard_map/reduce_scatter | solution.py:81
  147.2 1.2 copy-start.14
  147.2 160.5 %reduce-scatter.6.cloned.1.call-start = ((), (), s32[]{:S(2)}) async-start(), calls=%async_computation.5 | async-start | bytes 4718592 | tf_op jit(solution)/shard_map/reduce_scatter | solution.py:79
  153.8 1.0 copy-start.17
  153.9 246.0 %reduce-scatter.10.cloned.1.call-start = ((), (), s32[]{:S(2)}) async-start(), calls=%async_computation.9 | async-start | bytes 4718592 | tf_op jit(solution)/shard_map/reduce_scatter | solution.py:80
  157.6 306.1 %all-reduce.13.cloned.1.call-start = ((), (), s32[]{:S(2)}) async-start(), calls=%async_computation.17 | async-start | bytes 5242880 | tf_op jit(solution)/shard_map/psum | solution.py:83
  403.1 181.6 %all-reduce.11.cloned.1.call-start = ((), (), s32[]{:S(2)}) async-start(), calls=%async_computation.16 | async-start | bytes 5242880 | tf_op jit(solution)/shard_map/psum | solution.py:83
  463.7 188.9 %all-gather.6.cloned.1.call-start = ((), (), s32[]{:S(2)}) async-start(), calls=%async_computation.6 | async-start | bytes 2359296 | tf_op jit(solution)/shard_map/all_gather | solution.py:88
  463.8 140.2 %copy-start.10 = (f32[256,256]{1,0:T(8,128)}, f32[256,256]{1,0:T(8,128)S(1)}, u32[]{:S(2)}) copy-start(f32[256,256]{1,0:T(8,128)S(1)} %fusion.38) | copy-start | bytes 786436
  584.6 3.6 copy-start.4
  584.6 5.2 copy-start.5
  600.9 1.2 copy-start.9
  602.1 2.6 copy-start.7
  603.9 90.3 %all-gather.12.cloned.1.call-start = ((), (), s32[]{:S(2)}) async-start(), calls=%async_computation.12 | async-start | bytes 1179648 | tf_op jit(solution)/shard_map/all_gather | solution.py:90
  608.7 1.4 copy-start.11
  616.4 128.9 %all-gather.10.cloned.1.call-start = ((), (), s32[]{:S(2)}) async-start(), calls=%async_computation.10 | async-start | bytes 2359296 | tf_op jit(solution)/shard_map/all_gather | solution.py:89
  623.4 1.2 copy-start.8
  626.5 151.9 %reduce-scatter.8.cloned.1.call-start = ((), (), s32[]{:S(2)}) async-start(), calls=%async_computation.7 | async-start | bytes 2621440 | tf_op jit(solution)/shard_map/reduce_scatter | solution.py:97
  658.1 194.0 %reduce-scatter.14.cloned.1.call-start = ((), (), s32[]{:S(2)}) async-start(), calls=%async_computation.13 | async-start | bytes 10240000 | tf_op jit(solution)/shard_map/reduce_scatter | solution.py:99
  707.9 1.0 copy-start.15
  707.9 1.2 copy-start.16
  707.9 37.4 %copy-start.3 = (bf16[4,128,1024]{2,1,0:T(8,128)(2,1)S(1)}, bf16[4,128,1024]{2,1,0:T(8,128)(2,1)}, u32[]{:S(2)}) copy-start(bf16[4,128,1024]{2,1,0:T(8,128)(2,1)} %param.21) | copy-start | bytes 3145732
  707.9 180.2 %all-reduce.9.cloned.1.call-start = ((), (), s32[]{:S(2)}) async-start(), calls=%async_computation.15 | async-start | bytes 1048576
  748.8 158.4 %all-gather.8.cloned.1.call-start = ((), (), s32[]{:S(2)}) async-start(), calls=%async_computation.8 | async-start | bytes 1310720 | tf_op jit(solution)/shard_map/all_gather | solution.py:105
  780.6 77.5 %copy-start.21 = (u32[32]{0:T(128)S(1)}, u32[32]{0:T(128)}, u32[]{:S(2)}) copy-start(u32[32]{0:T(128)} %constant.11) | copy-start | bytes 388
  780.7 107.5 %copy-start.18 = (f32[4,32,256]{2,1,0:T(8,128)S(1)}, f32[4,32,256]{2,1,0:T(8,128)}, u32[]{:S(2)}) copy-start(f32[4,32,256]{2,1,0:T(8,128)} %param.22) | copy-start | bytes 393220
  780.7 107.5 %copy-start.19 = (f32[4,32,256]{2,1,0:T(8,128)S(1)}, f32[4,32,256]{2,1,0:T(8,128)}, u32[]{:S(2)}) copy-start(f32[4,32,256]{2,1,0:T(8,128)} %param.23) | copy-start | bytes 393220
  780.7 162.4 %all-gather.14.cloned.1.call-start = ((), (), s32[]{:S(2)}) async-start(), calls=%async_computation.14 | async-start | bytes 5120000 | tf_op jit(solution)/shard_map/all_gather | solution.py:107
  858.1 38.6 %copy-start.6 = (bf16[4,1024,256]{2,1,0:T(8,128)(2,1)S(1)}, bf16[4,1024,256]{2,1,0:T(8,128)(2,1)}, u32[]{:S(2)}) copy-start(bf16[4,1024,256]{2,1,0:T(8,128)(2,1)} %all-gather.10.cloned.1.call-done) | copy-start | bytes 6291460
  899.7 7.4 copy-start.13
  901.7 41.4 %copy-start.20 = (bf16[2,1024,256]{2,1,0:T(8,128)(2,1)S(1)}, bf16[2,1024,256]{2,1,0:T(8,128)(2,1)}, u32[]{:S(2)}) copy-start(bf16[2,1024,256]{2,1,0:T(8,128)(2,1)} %all-gather.12.cloned.1.call-done) | copy-start | bytes 3145732
  943.1 13.3 %copy-start.1 = (bf16[4,1024,256]{2,1,0:T(8,128)(2,1)S(1)}, bf16[4,1024,256]{2,1,0:T(8,128)(2,1)}, u32[]{:S(2)}) copy-start(bf16[4,1024,256]{2,1,0:T(8,128)(2,1)} %param.19) | copy-start | bytes 6291460
Sparse Core Ops, SparseCore 0:
  26.0 108.2 all-reduce.14
  147.3 68.2 reduce-scatter.11
  220.2 87.4 reduce-scatter.5
  311.7 88.0 reduce-scatter.9
  403.5 60.0 all-reduce.12
  467.9 116.6 all-reduce.10
  604.1 48.4 all-gather.5
  655.5 38.6 all-gather.11
  697.2 48.0 all-gather.9
  748.4 29.9 reduce-scatter.7
  781.6 70.5 reduce-scatter.13
  854.9 33.2 all-reduce.8
  890.3 16.8 all-gather.7
  909.1 33.9 all-gather.13
